TPU v7x, 256 devices: a whole 4x4x8 slice. The times are simulated.
256 devices in a mesh: lon: 64 (over x_hi, z, y), lat: 4 (over x_lo, core).
Axes of the slice: x: 4 (x_hi: 2, x_lo: 2; x = x_hi * 2 + x_lo), y: 4, z: 8, core: 2. Of those that a mesh axis runs over, the one named last changes fastest.
Arguments:
- thermal_anomaly: float32 [25, 64, 65536], P(None, 'lat', 'lon'), may hold values from -6 to 6
- saltiness_anomaly: float32 [25, 64, 65536], P(None, 'lat', 'lon'), may hold values from -6 to 6
- zonal_velocity_array: float32 [25, 64, 65536], P(None, 'lat', 'lon'), may hold values from -6 to 6
- meridional_velocity_array: float32 [25, 64, 65536], P(None, 'lat', 'lon'), may hold values from -6 to 6
- seawater_profile_flags: int32 [64, 65536], P('lat', 'lon'), may hold values 0 or 1
- submerged_layer_total: int32 [64, 65536], P('lat', 'lon'), may hold values from 0 to 25
- computed_block_flags: int32 [4, 64], P('lat', 'lon'), may hold values 0 or 1
Outputs:
- next_temperature: float32 [25, 64, 65536], P(None, 'lat', 'lon')
- next_salinity: float32 [25, 64, 65536], P(None, 'lat', 'lon')
- next_zonal: float32 [25, 64, 65536], P(None, 'lat', 'lon')
- next_meridional: float32 [25, 64, 65536], P(None, 'lat', 'lon')
All inputs are finite; a program needn't handle non-finite values. No bound on the sum of `seawater_profile_flags` or of `computed_block_flags` on one device may be relied on, other than what follows from the above.
Results may differ from a plain program's by a relative error of at most 0.00002.
Values sent between devices are 32-bit elements; how exact they have to be, the bound alone decides.
No kernel may reach another device: no remote copies, remote signals or barrier semaphores. Data moves between devices by JAX's collectives and lax.ppermute only.
A program may use at most 192 MiB of HBM per device.

v0:
```python
import jax
import jax.numpy as jnp
from jax import lax
from jax.sharding import PartitionSpec as P

ALPHA = 0.2
BETA = 0.8
GRAV_DZ = 0.1
DT_STEP = 0.2
VISC_TWO = 0.1
VISC_FOUR = 0.05
CORIOLIS_MAX = 0.3


def with_halo(value, sides, width, wrap):
    for axis, dim in sides:
        count, length = (lax.axis_size(axis), value.shape[dim])
        up = [(i, (i + 1) % count) for i in range(count if wrap else count - 1)]
        down = [(j, i) for i, j in up]
        last = lax.slice_in_dim(value, length - width, length, axis=dim)
        first = lax.slice_in_dim(value, 0, width, axis=dim)
        before = lax.ppermute(last, axis, up)
        after = lax.ppermute(first, axis, down)
        value = jnp.concatenate([before, value, after], axis=dim)
    return value


def from_partner(value, axis, distance):
    mask = 2**distance
    pairs = [(source, source ^ mask) for source in range(lax.axis_size(axis))]
    return lax.ppermute(value, axis, pairs)


def laplace(field):
    return (
        field[..., 2:, 1:-1]
        + field[..., :-2, 1:-1]
        + field[..., 1:-1, 2:]
        + field[..., 1:-1, :-2]
        - 4.0 * field[..., 1:-1, 1:-1]
    )


def update_fields(extended, submerged_share, coriolis):
    temper = extended[0]
    saline = extended[1]
    eastward = extended[2]
    northward = extended[3]
    density = BETA * saline - ALPHA * temper
    pressure = GRAV_DZ * (jnp.cumsum(density, axis=0) - 0.5 * density)
    laplacian = laplace(extended)
    bilaplacian = laplace(laplacian)
    centre = extended[..., 2:-2, 2:-2]
    mixing = VISC_TWO * laplacian[..., 1:-1, 1:-1] - VISC_FOUR * bilaplacian
    grad_east = 0.5 * (pressure[:, 2:-2, 3:-1] - pressure[:, 2:-2, 1:-3])
    grad_north = 0.5 * (pressure[:, 3:-1, 2:-2] - pressure[:, 1:-3, 2:-2])
    tracers = extended[0:2]
    flux_east = tracers * eastward
    flux_north = tracers * northward
    advection = 0.5 * (flux_east[..., 2:-2, 3:-1] - flux_east[..., 2:-2, 1:-3]) + 0.5 * (
        flux_north[..., 3:-1, 2:-2] - flux_north[..., 1:-3, 2:-2]
    )
    accel_east = coriolis * centre[3] - grad_east
    accel_north = -coriolis * centre[2] - grad_north
    forcing = jnp.concatenate([-advection, accel_east[None], accel_north[None]], axis=0)
    return submerged_share * (centre + DT_STEP * (forcing + mixing))


def per_device(
    thermal_anomaly,
    saltiness_anomaly,
    zonal_velocity_array,
    meridional_velocity_array,
    seawater_profile_flags,
    submerged_layer_total,
    computed_block_flags,
):
    block_depth_layers = thermal_anomaly.shape[0]
    block_meridional_extent = thermal_anomaly.shape[1]
    tile_alive = computed_block_flags[0, 0] == 1
    depth_index = jnp.arange(block_depth_layers, dtype=jnp.int32)[:, None, None]
    submerged_share = (
        (depth_index < submerged_layer_total[None])
        & (seawater_profile_flags[None] == 1)
        & tile_alive
    ).astype(jnp.float32)
    evolving_state_arrays = (
        jnp.stack(
            [thermal_anomaly, saltiness_anomaly, zonal_velocity_array, meridional_velocity_array]
        )
        * submerged_share
    )
    widened = with_halo(evolving_state_arrays, (("lon", 3),), 2, True)
    padded = with_halo(widened, (("lat", 2),), 2, False)
    signs = jnp.array([1.0, 1.0, -1.0, -1.0], jnp.float32).reshape(4, 1, 1, 1)
    strip = widened[:, :, -1:-3:-1, ::-1] * signs
    mirrored = strip
    for which_bit in range(lax.axis_size("lon").bit_length() - 1):
        mirrored = from_partner(mirrored, "lon", which_bit)
    is_northern = lax.axis_index("lat") == lax.axis_size("lat") - 1
    north_ghost = jnp.where(is_northern, mirrored, padded[:, :, -2:, :])
    extended = jnp.concatenate([padded[:, :, :-2, :], north_ghost], axis=2)
    total_rows = block_meridional_extent * lax.axis_size("lat")
    row_pos = (
        lax.axis_index("lat") * block_meridional_extent
        + jnp.arange(block_meridional_extent, dtype=jnp.int32)
    ).astype(jnp.float32)
    coriolis = (CORIOLIS_MAX * jnp.sin(jnp.pi * ((row_pos + 0.5) / total_rows - 0.5)))[:, None]
    updated = update_fields(extended, submerged_share, coriolis)
    return (updated[0], updated[1], updated[2], updated[3])


def solution(mesh):
    return jax.shard_map(
        per_device,
        mesh=mesh,
        in_specs=(
            P(None, "lat", "lon"),
            P(None, "lat", "lon"),
            P(None, "lat", "lon"),
            P(None, "lat", "lon"),
            P("lat", "lon"),
            P("lat", "lon"),
            P("lat", "lon"),
        ),
        out_specs=(
            P(None, "lat", "lon"),
            P(None, "lat", "lon"),
            P(None, "lat", "lon"),
            P(None, "lat", "lon"),
        ),
        check_vma=False,
    )
```

profile of v0, /device:TPU:14, one launch (start us, length us, event | category | flops | bytes accessed | tf_op | source)
XLA Modules:
  0.0 349.7 jit_solution(15509871856443452128)
XLA Ops:
  3.3 3.4 maximum_multiply_fusion
  6.7 2.7 copy-done.1
  17.0 7.6 %collective-permute-done = f32[4,25,16,2]{1,2,3,0:T(8,128)S(1)} collective-permute-done((f32[4,25,16,2]{1,2,3,0:T(8,128)S(1)}, f32[4,25,16,2]{1,2,3,0:T(8,128)S(1)}, u32[]{:S(2)}, u32[]{:S(2)}) %collective-permute-start) | collective-permute-done | bytes 12832 | tf_op jit(solution)/shard_map/ppermute | solution.py:22
  26.0 9.4 %concatenate.16 = f32[4,25,16,1028]{3,2,1,0:T(8,128)} concatenate(f32[4,25,16,2]{3,2,1,0:T(8,128)} %copy.14, f32[4,25,16,1024]{3,2,1,0:T(8,128)} %copy-done.1, f32[4,25,16,2]{3,2,1,0:T(8,128)S(1)} %copy.15), dimensions={3} | concatenate | bytes 13158400 | tf_op jit(solution)/shard_map/concatenate | solution.py:24
  35.4 4.7 %fusion.30 = (f32[4,25,2,1028]{3,2,1,0:T(2,128)}, f32[4,25,2,1028]{3,2,1,0:T(2,128)S(1)}) fusion(f32[4,25,16,1028]{3,2,1,0:T(8,128)} %concatenate.16), kind=kLoop, calls=%fused_computation.61 | loop fusion | bytes 3289600 | tf_op jit(solution)/shard_map/slice | solution.py:21
  40.1 5.3 %reverse = f32[4,25,2,1152]{3,2,1,0:T(2,128)} reverse(f32[4,25,2,1152]{3,2,1,0:T(2,128)S(1)} %bitcast.49), dimensions={2,3} | reverse | bytes 1843200
  47.6 7.8 %collective-permute-start.3 = (f32[4,25,2,1028]{3,2,1,0:T(2,128)S(1)}, f32[4,25,2,1028]{3,2,1,0:T(2,128)S(1)}, u32[]{:S(2)}, u32[]{:S(2)}) collective-permute-start(f32[4,25,2,1028]{3,2,1,0:T(2,128)S(1)} %broadcast_multiply_fusion), channel_id=1, source_target_pairs={{0,4},{4,0},{8,12},{12,8},{16,20},{20,16},{24,28},{28,24},{32,36},... | collective-permute-start | bytes 2467208 | tf_op jit(solution)/shard_map/ppermute | solution.py:31
  55.4 19.3 %collective-permute-done.3 = f32[4,25,2,1028]{3,2,1,0:T(2,128)S(1)} collective-permute-done((f32[4,25,2,1028]{3,2,1,0:T(2,128)S(1)}, f32[4,25,2,1028]{3,2,1,0:T(2,128)S(1)}, u32[]{:S(2)}, u32[]{:S(2)}) %collective-permute-start.3) | collective-permute-done | bytes 822432 | tf_op jit(solution)/shard_map/ppermute | solution.py:31
  74.7 21.4 %collective-permute-done.4 = f32[4,25,2,1028]{3,2,1,0:T(2,128)S(1)} collective-permute-done((f32[4,25,2,1028]{3,2,1,0:T(2,128)S(1)}, f32[4,25,2,1028]{3,2,1,0:T(2,128)S(1)}, u32[]{:S(2)}, u32[]{:S(2)}) %collective-permute-start.4) | collective-permute-done | bytes 822432 | tf_op jit(solution)/shard_map/ppermute | solution.py:31
  96.1 19.1 %collective-permute-done.5 = f32[4,25,2,1028]{3,2,1,0:T(2,128)S(1)} collective-permute-done((f32[4,25,2,1028]{3,2,1,0:T(2,128)S(1)}, f32[4,25,2,1028]{3,2,1,0:T(2,128)S(1)}, u32[]{:S(2)}, u32[]{:S(2)}) %collective-permute-start.5) | collective-permute-done | bytes 822432 | tf_op jit(solution)/shard_map/ppermute | solution.py:31
  115.2 78.5 %collective-permute-done.6 = f32[4,25,2,1028]{3,2,1,0:T(2,128)S(1)} collective-permute-done((f32[4,25,2,1028]{3,2,1,0:T(2,128)S(1)}, f32[4,25,2,1028]{3,2,1,0:T(2,128)S(1)}, u32[]{:S(2)}, u32[]{:S(2)}) %collective-permute-start.6) | collective-permute-done | bytes 822432 | tf_op jit(solution)/shard_map/ppermute | solution.py:31
  195.6 32.4 %collective-permute-done.7 = f32[4,25,2,1028]{3,2,1,0:T(2,128)} collective-permute-done((f32[4,25,2,1028]{3,2,1,0:T(2,128)S(1)}, f32[4,25,2,1028]{3,2,1,0:T(2,128)}, u32[]{:S(2)}, u32[]{:S(2)}) %collective-permute-start.7) | collective-permute-done | bytes 822432 | tf_op jit(solution)/shard_map/ppermute | solution.py:31
  228.0 11.4 %collective-permute-start.8 = (f32[4,25,2,1028]{3,2,1,0:T(2,128)}, f32[4,25,2,1028]{3,2,1,0:T(2,128)}, u32[]{:S(2)}, u32[]{:S(2)}) collective-permute-start(f32[4,25,2,1028]{3,2,1,0:T(2,128)} %collective-permute-done.7), channel_id=1, source_target_pairs={{0,128},{4,132},{8,136},{12,140},{16,144},{20,148},{24,152},{28,15... | collective-permute-start | bytes 2467208 | tf_op jit(solution)/shard_map/ppermute | solution.py:31
  241.6 17.9 %collective-permute-done.8 = f32[4,25,2,1028]{3,2,1,0:T(2,128)} collective-permute-done((f32[4,25,2,1028]{3,2,1,0:T(2,128)}, f32[4,25,2,1028]{3,2,1,0:T(2,128)}, u32[]{:S(2)}, u32[]{:S(2)}) %collective-permute-start.8) | collective-permute-done | bytes 822432 | tf_op jit(solution)/shard_map/ppermute | solution.py:31
  261.1 8.7 %collective-permute-done.2 = f32[4,25,2,1028]{3,2,1,0:T(2,128)} collective-permute-done((f32[4,25,2,1028]{3,2,1,0:T(2,128)S(1)}, f32[4,25,2,1028]{3,2,1,0:T(2,128)}, u32[]{:S(2)}, u32[]{:S(2)}) %collective-permute-start.2) | collective-permute-done | bytes 822432 | tf_op jit(solution)/shard_map/ppermute | solution.py:22
  269.9 5.0 %pad_maximum_fusion.2 = f32[4,25,20,1028]{3,2,1,0:T(8,128)S(1)} fusion(f32[4,25,2,1028]{3,2,1,0:T(2,128)S(1)} %broadcast_select_fusion, f32[4,25,16,1028]{3,2,1,0:T(8,128)} %concatenate.16, f32[4,25,2,1028]{3,2,1,0:T(2,128)} %collective-permute-done.2), kind=kLoop, calls=%fused_computation.7 | loop fusion | flops 4112000 | bytes 16448000 | tf_op jit(solution)/shard_map/concatenate | solution.py:102
  276.0 3.1 copy-done
  279.1 2.7 slice_bitcast_fusion.1
  281.8 9.0 %slice_multiply_fusion.2 = (f32[2,25,20,1028]{3,2,1,0:T(8,128)}, f32[2,25,20,1028]{3,2,1,0:T(8,128)}) fusion(f32[4,25,20,1028]{3,2,1,0:T(8,128)} %copy-done, f32[25,20,1028]{2,1,0:T(8,128)} %get-tuple-element.6, f32[25,20,1028]{2,1,0:T(8,128)} %get-tuple-element.7), kind=kLoop, calls=%fused_computation.20 | loop fusion | flops 2056000 | bytes 16448000 | tf_op jit(solution)/shard_map/mul | solution.py:58
  290.8 14.3 %fusion.11 = f32[2,25,16,1024]{3,2,1,0:T(8,128)} fusion(f32[2,25,20,1028]{3,2,1,0:T(8,128)} %get-tuple-element.5, f32[2,25,20,1028]{3,2,1,0:T(8,128)} %get-tuple-element.4), kind=kLoop, calls=%fused_computation.24 | loop fusion | flops 4096000 | bytes 16384000 | tf_op jit(solution)/shard_map/neg | solution.py:65
  305.1 5.7 %fusion.20 = (f32[1,25,16,1024]{3,2,1,0:T(8,128)}, f32[1,25,16,1024]{3,2,1,0:T(8,128)}) fusion(f32[25,20,1028]{2,1,0:T(8,128)S(1)} %subtract_multiply_fusion, f32[4,25,16,1024]{3,2,1,0:T(8,128)} %copy-done.1, f32[16]{0:T(128)S(1)} %get-tuple-element.18, f32[16]{0:T(128)S(1)} %get-tuple-element.19), kind=kLoop, calls=%fused_computation.46 | loop fusion | flops 3276800 | bytes 13107328 | tf_op jit(solution)/shard_map/broadcast_in_dim | solution.py:65
  310.7 26.9 %fusion = f32[4,25,18,1026]{3,2,1,0:T(8,128)S(1)} fusion(f32[4,25,20,1028]{3,2,1,0:T(8,128)} %copy-done, f32[4,25,16,1028]{3,2,1,0:T(8,128)} %concatenate.16, f32[4,25,2,1028]{3,2,1,0:T(2,128)} %collective-permute-done.2, f32[4,25,2,1028]{3,2,1,0:T(2,128)S(1)} %copy-done.4), kind=kLoop, calls=%fused_computation.1 | loop fusion | flops 12927600 | bytes 37772800 | tf_op jit(solution)/shard_map/sub | solution.py:36
  337.7 9.1 %fusion.8 = f32[4,25,16,1024]{3,2,1,0:T(8,128)S(1)} fusion(f32[4,25,18,1026]{3,2,1,0:T(8,128)S(1)} %fusion, f32[1,25,16,1024]{3,2,1,0:T(8,128)} %get-tuple-element.9, f32[1,25,16,1024]{3,2,1,0:T(8,128)} %get-tuple-element.8, f32[2,25,16,1024]{3,2,1,0:T(8,128)S(1)} %copy-done.2, f32[25,16,1024]{2,1,0:T(8,128)S(1)} %fusion.24, ...), kind=kLoop, calls=%fused_computation.15 | loop fusion | flops 29491200 | bytes 54067200 | tf_op jit(solution)/shard_map/mul | solution.py:66
  346.8 2.9 slice_bitcast_fusion.2
  (31 shorter events, 20.1 us)
Async XLA Ops:
  6.6 2.7 copy-start.1
  12.2 4.3 %collective-permute-start.1 = (f32[4,25,16,2]{1,2,3,0:T(8,128)S(1)}, f32[4,25,16,2]{1,2,3,0:T(8,128)S(1)}, u32[]{:S(2)}, u32[]{:S(2)}) collective-permute-start(f32[4,25,16,2]{1,2,3,0:T(8,128)S(1)} %copy.13), channel_id=1, source_target_pairs={{4,0},{8,4},{12,8},{16,12},{20,16},{24,20},{28,24},{32,28},{36,32}... | collective-permute-start | bytes 38408 | tf_op jit(solution)/shard_map/ppermute | solution.py:23
  13.2 11.4 %collective-permute-start = (f32[4,25,16,2]{1,2,3,0:T(8,128)S(1)}, f32[4,25,16,2]{1,2,3,0:T(8,128)S(1)}, u32[]{:S(2)}, u32[]{:S(2)}) collective-permute-start(f32[4,25,16,2]{1,2,3,0:T(8,128)S(1)} %copy.12), channel_id=1, source_target_pairs={{0,4},{4,8},{8,12},{12,16},{16,20},{20,24},{24,28},{28,32},{32,36}... | collective-permute-start | bytes 38408 | tf_op jit(solution)/shard_map/ppermute | solution.py:22
  35.4 10.0 %copy-start.5 = (f32[4]{0:T(128)S(1)}, f32[4]{0:T(128)}, u32[]{:S(2)}) copy-start(f32[4]{0:T(128)} %constant.46.clone) | copy-start | bytes 52
  47.6 27.1 %collective-permute-start.3 = (f32[4,25,2,1028]{3,2,1,0:T(2,128)S(1)}, f32[4,25,2,1028]{3,2,1,0:T(2,128)S(1)}, u32[]{:S(2)}, u32[]{:S(2)}) collective-permute-start(f32[4,25,2,1028]{3,2,1,0:T(2,128)S(1)} %broadcast_multiply_fusion), channel_id=1, source_target_pairs={{0,4},{4,0},{8,12},{12,8},{16,20},{20,16},{24,28},{28,24},{32,36},... | collective-permute-start | bytes 2467208 | tf_op jit(solution)/shard_map/ppermute | solution.py:31
  74.7 21.4 %collective-permute-start.4 = (f32[4,25,2,1028]{3,2,1,0:T(2,128)S(1)}, f32[4,25,2,1028]{3,2,1,0:T(2,128)S(1)}, u32[]{:S(2)}, u32[]{:S(2)}) collective-permute-start(f32[4,25,2,1028]{3,2,1,0:T(2,128)S(1)} %collective-permute-done.3), channel_id=1, source_target_pairs={{0,8},{4,12},{8,0},{12,4},{16,24},{20,28},{24,16},{28,20},{32,40},... | collective-permute-start | bytes 2467208 | tf_op jit(solution)/shard_map/ppermute | solution.py:31
  96.1 19.1 %collective-permute-start.5 = (f32[4,25,2,1028]{3,2,1,0:T(2,128)S(1)}, f32[4,25,2,1028]{3,2,1,0:T(2,128)S(1)}, u32[]{:S(2)}, u32[]{:S(2)}) collective-permute-start(f32[4,25,2,1028]{3,2,1,0:T(2,128)S(1)} %collective-permute-done.4), channel_id=1, source_target_pairs={{0,16},{4,20},{8,24},{12,28},{16,0},{20,4},{24,8},{28,12},{32,48},... | collective-permute-start | bytes 2467208 | tf_op jit(solution)/shard_map/ppermute | solution.py:31
  115.2 78.5 %collective-permute-start.6 = (f32[4,25,2,1028]{3,2,1,0:T(2,128)S(1)}, f32[4,25,2,1028]{3,2,1,0:T(2,128)S(1)}, u32[]{:S(2)}, u32[]{:S(2)}) collective-permute-start(f32[4,25,2,1028]{3,2,1,0:T(2,128)S(1)} %collective-permute-done.5), channel_id=1, source_target_pairs={{0,32},{4,36},{8,40},{12,44},{16,48},{20,52},{24,56},{28,60},{32,0... | collective-permute-start | bytes 2467208 | tf_op jit(solution)/shard_map/ppermute | solution.py:31
  193.7 34.3 %collective-permute-start.7 = (f32[4,25,2,1028]{3,2,1,0:T(2,128)S(1)}, f32[4,25,2,1028]{3,2,1,0:T(2,128)}, u32[]{:S(2)}, u32[]{:S(2)}) collective-permute-start(f32[4,25,2,1028]{3,2,1,0:T(2,128)S(1)} %collective-permute-done.6), channel_id=1, source_target_pairs={{0,64},{4,68},{8,72},{12,76},{16,80},{20,84},{24,88},{28,92},{32,9... | collective-permute-start | bytes 2467208 | tf_op jit(solution)/shard_map/ppermute | solution.py:31
  193.7 47.9 %collective-permute-start.9 = (f32[4,25,2,1028]{3,2,1,0:T(2,128)}, f32[4,25,2,1028]{3,2,1,0:T(2,128)}, u32[]{:S(2)}, u32[]{:S(2)}) collective-permute-start(f32[4,25,2,1028]{3,2,1,0:T(2,128)} %get-tuple-element.10), channel_id=1, source_target_pairs={{1,0},{2,1},{3,2},{5,4},{6,5},{7,6},{9,8},{10,9},{11,10},{13,12},{... | collective-permute-start | bytes 2467208 | tf_op jit(solution)/shard_map/ppermute | solution.py:23
  228.0 31.4 %collective-permute-start.8 = (f32[4,25,2,1028]{3,2,1,0:T(2,128)}, f32[4,25,2,1028]{3,2,1,0:T(2,128)}, u32[]{:S(2)}, u32[]{:S(2)}) collective-permute-start(f32[4,25,2,1028]{3,2,1,0:T(2,128)} %collective-permute-done.7), channel_id=1, source_target_pairs={{0,128},{4,132},{8,136},{12,140},{16,144},{20,148},{24,152},{28,15... | collective-permute-start | bytes 2467208 | tf_op jit(solution)/shard_map/ppermute | solution.py:31
  239.4 30.4 %collective-permute-start.2 = (f32[4,25,2,1028]{3,2,1,0:T(2,128)S(1)}, f32[4,25,2,1028]{3,2,1,0:T(2,128)}, u32[]{:S(2)}, u32[]{:S(2)}) collective-permute-start(f32[4,25,2,1028]{3,2,1,0:T(2,128)S(1)} %get-tuple-element.11), channel_id=1, source_target_pairs={{0,1},{1,2},{2,3},{4,5},{5,6},{6,7},{8,9},{9,10},{10,11},{12,13},{... | collective-permute-start | bytes 2467208 | tf_op jit(solution)/shard_map/ppermute | solution.py:22
  261.1 13.8 %copy-start.3 = (f32[4,25,2,1028]{3,2,1,0:T(2,128)}, f32[4,25,2,1028]{3,2,1,0:T(2,128)S(1)}, u32[]{:S(2)}) copy-start(f32[4,25,2,1028]{3,2,1,0:T(2,128)S(1)} %broadcast_select_fusion) | copy-start | bytes 2467204
  274.9 4.2 %copy-start = (f32[4,25,20,1028]{3,2,1,0:T(8,128)}, f32[4,25,20,1028]{3,2,1,0:T(8,128)S(1)}, u32[]{:S(2)}) copy-start(f32[4,25,20,1028]{3,2,1,0:T(8,128)S(1)} %pad_maximum_fusion.2) | copy-start | bytes 24672004
  305.1 5.7 %copy-start.4 = (f32[4,25,2,1028]{3,2,1,0:T(2,128)S(1)}, f32[4,25,2,1028]{3,2,1,0:T(2,128)}, u32[]{:S(2)}) copy-start(f32[4,25,2,1028]{3,2,1,0:T(2,128)} %copy-done.3) | copy-start | bytes 2467204
  310.7 26.9 %copy-start.2 = (f32[2,25,16,1024]{3,2,1,0:T(8,128)S(1)}, f32[2,25,16,1024]{3,2,1,0:T(8,128)}, u32[]{:S(2)}) copy-start(f32[2,25,16,1024]{3,2,1,0:T(8,128)} %fusion.11) | copy-start | bytes 9830404
where the time goes:
time: 350 us
  waiting for transfers between devices  207 us (59%)
  other arithmetic  80.3 us (23%)
  local copies, waits for them, and re-layouts  36 us (10%)
  starting transfers between devices  25.4 us (7%)
    ppermute x6, waiting for transfers between devices, from_partner(): return lax.ppermute(value, axis, pairs)  189 us
    sub x1, other arithmetic, laplace(): field[..., 2:, 1:-1] + field[..., :-2, 1:-1] + field[..., 1:-1, 2:]  26.9 us
    ppermute x6, starting transfers between devices, from_partner(): return lax.ppermute(value, axis, pairs)  19.3 us
    ppermute x2, waiting for transfers between devices, with_halo(): before = lax.ppermute(last, axis, up)  16.3 us
    neg x1, other arithmetic, update_fields(): -advection  14.3 us
    unnamed x13, local copies, waits for them, and re-layouts  11 us
    concatenate x1, local copies, waits for them, and re-layouts, with_halo(): value = jnp.concatenate([before, value, after], axis=dim)  9.39 us
    mul x1, other arithmetic, update_fields(): return submerged_share * (centre + DT_STEP * (forcing + mixing))  9.1 us
  transfers between devices with their start and end apart: 10, of which 9 were waited for; matrix products, arithmetic and copies ran while one was open for 1% of the time, Pallas kernels for 0%

commit v1 on v0

--- a/solution.py
+++ b/solution.py
@@ -66,6 +66,17 @@
     return submerged_share * (centre + DT_STEP * (forcing + mixing))
 
 
+def shift_pairs(count, step, wrap):
+    pairs = []
+    for i in range(count):
+        j = i + step
+        if wrap:
+            pairs.append((i, j % count))
+        elif 0 <= j < count:
+            pairs.append((i, j))
+    return pairs
+
+
 def per_device(
     thermal_anomaly,
     saltiness_anomaly,
@@ -77,6 +88,8 @@
 ):
     block_depth_layers = thermal_anomaly.shape[0]
     block_meridional_extent = thermal_anomaly.shape[1]
+    n_lon = lax.axis_size("lon")
+    n_lat = lax.axis_size("lat")
     tile_alive = computed_block_flags[0, 0] == 1
     depth_index = jnp.arange(block_depth_layers, dtype=jnp.int32)[:, None, None]
     submerged_share = (
@@ -84,23 +97,28 @@
         & (seawater_profile_flags[None] == 1)
         & tile_alive
     ).astype(jnp.float32)
-    evolving_state_arrays = (
+    fields = (
         jnp.stack(
             [thermal_anomaly, saltiness_anomaly, zonal_velocity_array, meridional_velocity_array]
         )
         * submerged_share
     )
-    widened = with_halo(evolving_state_arrays, (("lon", 3),), 2, True)
-    padded = with_halo(widened, (("lat", 2),), 2, False)
+    top = fields[:, :, -2:, :]
+    bottom = fields[:, :, :2, :]
+    from_south = lax.ppermute(top, "lat", shift_pairs(n_lat, 1, False))
+    from_north = lax.ppermute(bottom, "lat", shift_pairs(n_lat, -1, False))
+    last = n_lat - 1
+    fold_pairs = [(p * n_lat + last, (n_lon - 1 - p) * n_lat + last) for p in range(n_lon)]
+    folded = lax.ppermute(top, ("lon", "lat"), fold_pairs)
     signs = jnp.array([1.0, 1.0, -1.0, -1.0], jnp.float32).reshape(4, 1, 1, 1)
-    strip = widened[:, :, -1:-3:-1, ::-1] * signs
-    mirrored = strip
-    for which_bit in range(lax.axis_size("lon").bit_length() - 1):
-        mirrored = from_partner(mirrored, "lon", which_bit)
-    is_northern = lax.axis_index("lat") == lax.axis_size("lat") - 1
-    north_ghost = jnp.where(is_northern, mirrored, padded[:, :, -2:, :])
-    extended = jnp.concatenate([padded[:, :, :-2, :], north_ghost], axis=2)
-    total_rows = block_meridional_extent * lax.axis_size("lat")
+    fold_rows = folded[:, :, ::-1, ::-1] * signs
+    is_northern = lax.axis_index("lat") == last
+    north = jnp.where(is_northern, fold_rows, from_north)
+    tall = jnp.concatenate([from_south, fields, north], axis=2)
+    west = lax.ppermute(tall[..., -2:], "lon", shift_pairs(n_lon, 1, True))
+    east = lax.ppermute(tall[..., :2], "lon", shift_pairs(n_lon, -1, True))
+    extended = jnp.concatenate([west, tall, east], axis=3)
+    total_rows = block_meridional_extent * n_lat
     row_pos = (
         lax.axis_index("lat") * block_meridional_extent
         + jnp.arange(block_meridional_extent, dtype=jnp.int32)

time: 350 us -> 166 us (0.47)
  the two profiles are of different devices: /device:TPU:14 before, /device:TPU:3 now
where the time goes in v1:
time: 166 us
  other arithmetic  78.8 us (47%)
  local copies, waits for them, and re-layouts  47.5 us (29%)
  starting transfers between devices  22.5 us (14%)
  waiting for transfers between devices  15.3 us (9%)
    sub x1, other arithmetic, laplace(): field[..., 2:, 1:-1] + field[..., :-2, 1:-1] + field[..., 1:-1, 2:]  29.1 us
    ppermute x1, waiting for transfers between devices, per_device(): folded = lax.ppermute(top, ('lon', 'lat'), fold_pairs)  15.3 us
    neg x1, other arithmetic, update_fields(): -advection  14.4 us
    concatenate x1, local copies, waits for them, and re-layouts, per_device(): extended = jnp.concatenate([west, tall, east], axis=3)  13.7 us
    ppermute x1, starting transfers between devices, per_device(): folded = lax.ppermute(top, ('lon', 'lat'), fold_pairs)  11.5 us
    mul x1, other arithmetic, update_fields(): return submerged_share * (centre + DT_STEP * (forcing + mixing))  9.56 us
    mul x1, other arithmetic, update_fields(): flux_east = tracers * eastward  8.94 us
    unnamed x16, local copies, waits for them, and re-layouts  8.31 us
  transfers between devices with their start and end apart: 5, of which 1 were waited for; matrix products, arithmetic and copies ran while one was open for 6% of the time, Pallas kernels for 0%

profile of v1, /device:TPU:3, one launch (start us, length us, event | category | flops | bytes accessed | tf_op | source)
XLA Modules:
  0.0 165.6 jit_solution(17467583444855898990)
XLA Ops:
  3.3 3.3 %maximum_multiply_fusion = f32[4,25,16,1024]{3,2,1,0:T(8,128)S(1)} fusion(f32[1,25,16,1024]{3,2,1,0:T(8,128)} %bitcast.40, f32[1,25,16,1024]{3,2,1,0:T(8,128)} %bitcast.42, f32[1,25,16,1024]{3,2,1,0:T(8,128)} %bitcast.44, f32[1,25,16,1024]{3,2,1,0:T(8,128)} %bitcast.46, f32[25,16,1024]{2,1,0:T(8,128)S(1)} %fusion.25), kind=kLoop, calls=%fused_computation.22 | loop fusion | flops 6553600 | bytes 14745600 | tf_op jit(solution)/shard_map/mul | solution.py:101
  6.6 2.7 %copy-done.1 = f32[4,25,16,1024]{3,2,1,0:T(8,128)} copy-done((f32[4,25,16,1024]{3,2,1,0:T(8,128)}, f32[4,25,16,1024]{3,2,1,0:T(8,128)S(1)}, u32[]{:S(2)}) %copy-start.1) | copy-done | bytes 6553624
  9.3 2.0 %fusion.32 = (f32[4,25,2,1024]{3,2,1,0:T(2,128)}, f32[4,25,2,1024]{3,2,1,0:T(2,128)}) fusion(f32[4,25,16,1024]{3,2,1,0:T(8,128)S(1)} %maximum_multiply_fusion), kind=kLoop, calls=%fused_computation.65 | loop fusion | bytes 3276800 | tf_op jit(solution)/shard_map/slice | solution.py:106
  11.3 11.5 %collective-permute-start.1 = (f32[4,25,2,1024]{3,2,1,0:T(2,128)}, f32[4,25,2,1024]{3,2,1,0:T(2,128)}, u32[]{:S(2)}, u32[]{:S(2)}) collective-permute-start(f32[4,25,2,1024]{3,2,1,0:T(2,128)} %get-tuple-element.16), channel_id=1, source_target_pairs={{3,255},{7,251},{11,247},{15,243},{19,239},{23,235},{27,231},{31,2... | collective-permute-start | bytes 2457608 | tf_op jit(solution)/shard_map/ppermute | solution.py:112
  22.8 2.2 %collective-permute-start.2 = (f32[4,25,2,1024]{3,2,1,0:T(2,128)}, f32[4,25,2,1024]{3,2,1,0:T(2,128)}, u32[]{:S(2)}, u32[]{:S(2)}) collective-permute-start(f32[4,25,2,1024]{3,2,1,0:T(2,128)} %get-tuple-element.17), channel_id=1, source_target_pairs={{1,0},{2,1},{3,2},{5,4},{6,5},{7,6},{9,8},{10,9},{11,10},{13,12},{... | collective-permute-start | bytes 2457608 | tf_op jit(solution)/shard_map/ppermute | solution.py:109
  26.4 15.3 %collective-permute-done.1 = f32[4,25,2,1024]{3,2,1,0:T(2,128)} collective-permute-done((f32[4,25,2,1024]{3,2,1,0:T(2,128)}, f32[4,25,2,1024]{3,2,1,0:T(2,128)}, u32[]{:S(2)}, u32[]{:S(2)}) %collective-permute-start.1) | collective-permute-done | bytes 819232 | tf_op jit(solution)/shard_map/ppermute | solution.py:112
  41.6 5.6 %rev.3 = f32[4,25,2,1024]{3,2,1,0:T(2,128)S(1)} reverse(f32[4,25,2,1024]{3,2,1,0:T(2,128)} %collective-permute-done.1), dimensions={2,3} | reverse | bytes 1638400 | tf_op jit(solution)/shard_map/rev | solution.py:114
  47.8 4.1 %pad_maximum_fusion.6 = f32[4,25,20,1024]{3,2,1,0:T(8,128)S(1)} fusion(f32[4,25,2,1024]{3,2,1,0:T(2,128)S(1)} %multiply_select_fusion, f32[4,25,16,1024]{3,2,1,0:T(8,128)} %copy-done.1, f32[4,25,2,1024]{3,2,1,0:T(2,128)} %collective-permute-done), kind=kLoop, calls=%fused_computation.11 | loop fusion | flops 4096000 | bytes 16384000 | tf_op jit(solution)/shard_map/concatenate | solution.py:117
  52.0 3.7 %copy-done.2 = f32[4,25,20,1024]{3,2,1,0:T(8,128)} copy-done((f32[4,25,20,1024]{3,2,1,0:T(8,128)}, f32[4,25,20,1024]{3,2,1,0:T(8,128)S(1)}, u32[]{:S(2)}) %copy-start.2) | copy-done | bytes 8192024
  55.7 1.9 %fusion.31 = (f32[4,25,20,2]{3,2,1,0:T(8,128)}, f32[4,25,20,2]{3,2,1,0:T(8,128)}) fusion(f32[4,25,20,1024]{3,2,1,0:T(8,128)S(1)} %pad_maximum_fusion.6), kind=kLoop, calls=%fused_computation.64 | loop fusion | bytes 64000 | tf_op jit(solution)/shard_map/slice | solution.py:119
  57.6 1.9 %copy.12 = f32[4,25,20,2]{1,0,3,2:T(4,128)S(1)} copy(f32[4,25,20,2]{3,2,1,0:T(8,128)} %get-tuple-element.9) | data formatting | bytes 32000 | tf_op jit(solution)/shard_map/slice | solution.py:118
  59.5 1.9 %copy.13 = f32[4,25,20,2]{1,0,3,2:T(4,128)S(1)} copy(f32[4,25,20,2]{3,2,1,0:T(8,128)} %get-tuple-element.8) | data formatting | bytes 32000 | tf_op jit(solution)/shard_map/slice | solution.py:119
  61.4 7.4 %collective-permute-start.4 = (f32[4,25,20,2]{1,0,3,2:T(4,128)S(1)}, f32[4,25,20,2]{1,0,3,2:T(4,128)S(1)}, u32[]{:S(2)}, u32[]{:S(2)}) collective-permute-start(f32[4,25,20,2]{1,0,3,2:T(4,128)S(1)} %copy.13), channel_id=1, source_target_pairs={{0,252},{4,0},{8,4},{12,8},{16,12},{20,16},{24,20},{28,24},{32,28}... | collective-permute-start | bytes 48008 | tf_op jit(solution)/shard_map/ppermute | solution.py:119
  68.8 1.7 %copy.14 = f32[4,25,20,2]{3,2,1,0:T(8,128)} copy(f32[4,25,20,2]{1,0,3,2:T(4,128)S(1)} %collective-permute-done.3) | data formatting | bytes 32000 | tf_op jit(solution)/shard_map/ppermute | solution.py:118
  70.6 1.7 %copy.15 = f32[4,25,20,2]{3,2,1,0:T(8,128)} copy(f32[4,25,20,2]{1,0,3,2:T(4,128)S(1)} %collective-permute-done.4) | data formatting | bytes 32000 | tf_op jit(solution)/shard_map/ppermute | solution.py:119
  72.3 13.7 %concatenate.16 = f32[4,25,20,1028]{3,2,1,0:T(8,128)} concatenate(f32[4,25,20,2]{3,2,1,0:T(8,128)} %copy.14, f32[4,25,20,1024]{3,2,1,0:T(8,128)} %copy-done.2, f32[4,25,20,2]{3,2,1,0:T(8,128)} %copy.15), dimensions={3} | concatenate | bytes 16448000 | tf_op jit(solution)/shard_map/concatenate | solution.py:120
  86.0 5.9 %slice_bitcast_fusion.1 = (f32[25,20,1028]{2,1,0:T(8,128)}, f32[25,20,1028]{2,1,0:T(8,128)}) fusion(f32[4,25,20,1028]{3,2,1,0:T(8,128)} %concatenate.16), kind=kLoop, calls=%fused_computation.35 | loop fusion | bytes 8224000 | tf_op jit(solution)/shard_map/mul | solution.py:58
  91.9 1.8 %copy-done = f32[4,25,20,1028]{3,2,1,0:T(8,128)S(1)} copy-done((f32[4,25,20,1028]{3,2,1,0:T(8,128)S(1)}, f32[4,25,20,1028]{3,2,1,0:T(8,128)}, u32[]{:S(2)}) %copy-start) | copy-done | bytes 8224024
  94.9 8.9 %slice_multiply_fusion.2 = (f32[2,25,20,1028]{3,2,1,0:T(8,128)}, f32[2,25,20,1028]{3,2,1,0:T(8,128)}) fusion(f32[4,25,20,1028]{3,2,1,0:T(8,128)} %concatenate.16, f32[25,20,1028]{2,1,0:T(8,128)} %get-tuple-element.6, f32[25,20,1028]{2,1,0:T(8,128)} %get-tuple-element.7), kind=kLoop, calls=%fused_computation.24 | loop fusion | flops 2056000 | bytes 16448000 | tf_op jit(solution)/shard_map/mul | solution.py:58
  103.8 14.4 %fusion.12 = f32[2,25,16,1024]{3,2,1,0:T(8,128)} fusion(f32[2,25,20,1028]{3,2,1,0:T(8,128)} %get-tuple-element.5, f32[2,25,20,1028]{3,2,1,0:T(8,128)} %get-tuple-element.4), kind=kLoop, calls=%fused_computation.28 | loop fusion | flops 4096000 | bytes 16384000 | tf_op jit(solution)/shard_map/neg | solution.py:65
  118.2 5.7 %fusion.21 = (f32[1,25,16,1024]{3,2,1,0:T(8,128)}, f32[1,25,16,1024]{3,2,1,0:T(8,128)}) fusion(f32[25,20,1028]{2,1,0:T(8,128)S(1)} %subtract_multiply_fusion, f32[4,25,16,1024]{3,2,1,0:T(8,128)} %copy-done.1, f32[16]{0:T(128)S(1)} %get-tuple-element.18, f32[16]{0:T(128)S(1)} %get-tuple-element.19), kind=kLoop, calls=%fused_computation.50 | loop fusion | flops 3276800 | bytes 13107328 | tf_op jit(solution)/shard_map/broadcast_in_dim | solution.py:65
  124.0 29.1 %fusion = f32[4,25,18,1026]{3,2,1,0:T(8,128)S(1)} fusion(f32[4,25,20,1028]{3,2,1,0:T(8,128)} %concatenate.16, f32[4,25,20,2]{3,2,1,0:T(8,128)S(1)} %copy-done.3, f32[4,25,2,1024]{3,2,1,0:T(2,128)S(1)} %copy-done.6, f32[4,25,16,1024]{3,2,1,0:T(8,128)} %copy-done.1, f32[4,25,2,1024]{3,2,1,0:T(2,128)} %collective-permute-done, f32[4,25,20,2]{3,2,1,0:T(8,128)S(1)} %copy-done.4), kind=kLoop, calls=%fused_computation.1 | loop fusion | flops 20314800 | bytes 37772800 | tf_op jit(solution)/shard_map/sub | solution.py:36
  153.1 9.6 %fusion.9 = f32[4,25,16,1024]{3,2,1,0:T(8,128)S(1)} fusion(f32[4,25,18,1026]{3,2,1,0:T(8,128)S(1)} %fusion, f32[1,25,16,1024]{3,2,1,0:T(8,128)} %get-tuple-element.11, f32[1,25,16,1024]{3,2,1,0:T(8,128)} %get-tuple-element.10, f32[2,25,16,1024]{3,2,1,0:T(8,128)} %fusion.12, f32[25,16,1024]{2,1,0:T(8,128)S(1)} %fusion.25, f32[1,25,16,1024]{3,2,1,0:T(8,128)} %bitcast.41, ...), kind=kLoop, calls=%fused_computation.19 | loop fusion | flops 29491200 | bytes 54067200 | tf_op jit(solution)/shard_map/mul | solution.py:66
  162.7 2.9 %slice_bitcast_fusion.2 = (f32[25,16,1024]{2,1,0:T(8,128)}, f32[25,16,1024]{2,1,0:T(8,128)}, f32[25,16,1024]{2,1,0:T(8,128)}, f32[25,16,1024]{2,1,0:T(8,128)}) fusion(f32[4,25,16,1024]{3,2,1,0:T(8,128)S(1)} %fusion.9), kind=kLoop, calls=%fused_computation.37 | loop fusion | bytes 13107200 | tf_op jit(solution)/shard_map/squeeze | solution.py:128
  (24 shorter events, 5.0 us)
Async XLA Ops:
  3.2 44.0 %copy-start.7 = (f32[4]{0:T(128)S(1)}, f32[4]{0:T(128)}, u32[]{:S(2)}) copy-start(f32[4]{0:T(128)} %constant.46.clone) | copy-start | bytes 52
  6.6 2.7 %copy-start.1 = (f32[4,25,16,1024]{3,2,1,0:T(8,128)}, f32[4,25,16,1024]{3,2,1,0:T(8,128)S(1)}, u32[]{:S(2)}) copy-start(f32[4,25,16,1024]{3,2,1,0:T(8,128)S(1)} %maximum_multiply_fusion) | copy-start | bytes 19660804
  11.3 30.3 %collective-permute-start.1 = (f32[4,25,2,1024]{3,2,1,0:T(2,128)}, f32[4,25,2,1024]{3,2,1,0:T(2,128)}, u32[]{:S(2)}, u32[]{:S(2)}) collective-permute-start(f32[4,25,2,1024]{3,2,1,0:T(2,128)} %get-tuple-element.16), channel_id=1, source_target_pairs={{3,255},{7,251},{11,247},{15,243},{19,239},{23,235},{27,231},{31,2... | collective-permute-start | bytes 2457608 | tf_op jit(solution)/shard_map/ppermute | solution.py:112
  22.8 24.4 %collective-permute-start.2 = (f32[4,25,2,1024]{3,2,1,0:T(2,128)}, f32[4,25,2,1024]{3,2,1,0:T(2,128)}, u32[]{:S(2)}, u32[]{:S(2)}) collective-permute-start(f32[4,25,2,1024]{3,2,1,0:T(2,128)} %get-tuple-element.17), channel_id=1, source_target_pairs={{1,0},{2,1},{3,2},{5,4},{6,5},{7,6},{9,8},{10,9},{11,10},{13,12},{... | collective-permute-start | bytes 2457608 | tf_op jit(solution)/shard_map/ppermute | solution.py:109
  25.1 22.7 %collective-permute-start = (f32[4,25,2,1024]{3,2,1,0:T(2,128)}, f32[4,25,2,1024]{3,2,1,0:T(2,128)}, u32[]{:S(2)}, u32[]{:S(2)}) collective-permute-start(f32[4,25,2,1024]{3,2,1,0:T(2,128)} %get-tuple-element.16), channel_id=1, source_target_pairs={{0,1},{1,2},{2,3},{4,5},{5,6},{6,7},{8,9},{9,10},{10,11},{12,13},{... | collective-permute-start | bytes 2457608 | tf_op jit(solution)/shard_map/ppermute | solution.py:108
  47.8 4.2 %copy-start.5 = (f32[4,25,2,1024]{3,2,1,0:T(2,128)}, f32[4,25,2,1024]{3,2,1,0:T(2,128)S(1)}, u32[]{:S(2)}) copy-start(f32[4,25,2,1024]{3,2,1,0:T(2,128)S(1)} %multiply_select_fusion) | copy-start | bytes 2457604
  51.9 3.7 %copy-start.2 = (f32[4,25,20,1024]{3,2,1,0:T(8,128)}, f32[4,25,20,1024]{3,2,1,0:T(8,128)S(1)}, u32[]{:S(2)}) copy-start(f32[4,25,20,1024]{3,2,1,0:T(8,128)S(1)} %pad_maximum_fusion.6) | copy-start | bytes 24576004
  59.4 9.4 %collective-permute-start.3 = (f32[4,25,20,2]{1,0,3,2:T(4,128)S(1)}, f32[4,25,20,2]{1,0,3,2:T(4,128)S(1)}, u32[]{:S(2)}, u32[]{:S(2)}) collective-permute-start(f32[4,25,20,2]{1,0,3,2:T(4,128)S(1)} %copy.12), channel_id=1, source_target_pairs={{0,4},{4,8},{8,12},{12,16},{16,20},{20,24},{24,28},{28,32},{32,36}... | collective-permute-start | bytes 48008 | tf_op jit(solution)/shard_map/ppermute | solution.py:118
  61.4 9.2 %collective-permute-start.4 = (f32[4,25,20,2]{1,0,3,2:T(4,128)S(1)}, f32[4,25,20,2]{1,0,3,2:T(4,128)S(1)}, u32[]{:S(2)}, u32[]{:S(2)}) collective-permute-start(f32[4,25,20,2]{1,0,3,2:T(4,128)S(1)} %copy.13), channel_id=1, source_target_pairs={{0,252},{4,0},{8,4},{12,8},{16,12},{20,16},{24,20},{28,24},{32,28}... | collective-permute-start | bytes 48008 | tf_op jit(solution)/shard_map/ppermute | solution.py:119
  86.0 7.8 %copy-start = (f32[4,25,20,1028]{3,2,1,0:T(8,128)S(1)}, f32[4,25,20,1028]{3,2,1,0:T(8,128)}, u32[]{:S(2)}) copy-start(f32[4,25,20,1028]{3,2,1,0:T(8,128)} %concatenate.16) | copy-start | bytes 24672004
  118.2 5.8 %copy-start.3 = (f32[4,25,20,2]{3,2,1,0:T(8,128)S(1)}, f32[4,25,20,2]{3,2,1,0:T(8,128)}, u32[]{:S(2)}) copy-start(f32[4,25,20,2]{3,2,1,0:T(8,128)} %copy.14) | copy-start | bytes 48004
  118.2 5.8 %copy-start.4 = (f32[4,25,20,2]{3,2,1,0:T(8,128)S(1)}, f32[4,25,20,2]{3,2,1,0:T(8,128)}, u32[]{:S(2)}) copy-start(f32[4,25,20,2]{3,2,1,0:T(8,128)} %copy.15) | copy-start | bytes 48004
  118.2 5.8 %copy-start.6 = (f32[4,25,2,1024]{3,2,1,0:T(2,128)S(1)}, f32[4,25,2,1024]{3,2,1,0:T(2,128)}, u32[]{:S(2)}) copy-start(f32[4,25,2,1024]{3,2,1,0:T(2,128)} %copy-done.5) | copy-start | bytes 2457604

commit v2 on v1

--- a/solution.py
+++ b/solution.py
@@ -2,6 +2,8 @@
 import jax.numpy as jnp
 from jax import lax
 from jax.sharding import PartitionSpec as P
+from jax.experimental import pallas as pl
+from jax.experimental.pallas import tpu as pltpu
 
 ALPHA = 0.2
 BETA = 0.8
@@ -66,6 +68,113 @@
     return submerged_share * (centre + DT_STEP * (forcing + mixing))
 
 
+RING_ROWS = 24
+RING_COLS = 128
+
+
+def _lap(a):
+    rows, cols = a.shape
+    return (
+        pltpu.roll(a, rows - 1, 0)
+        + pltpu.roll(a, 1, 0)
+        + pltpu.roll(a, cols - 1, 1)
+        + pltpu.roll(a, 1, 1)
+        - 4.0 * a
+    )
+
+
+def _step_kernel(levels_ref, cor_ref, t_ref, s_ref, u_ref, v_ref, rows_ref, side_ref,
+                 ot_ref, os_ref, ou_ref, ov_ref, ext_ref, cum_ref):
+    k = pl.program_id(0)
+    ny, nx = t_ref.shape[1], t_ref.shape[2]
+
+    @pl.when(k == 0)
+    def _():
+        cum_ref[...] = jnp.zeros_like(cum_ref)
+
+    wet = (levels_ref[...] > k).astype(jnp.float32)
+    for c, ref in enumerate((t_ref, s_ref, u_ref, v_ref)):
+        ext_ref[c, 0:ny, 0:nx] = ref[0] * wet
+        ext_ref[c, ny:RING_ROWS, 0:nx] = rows_ref[0, c]
+        ext_ref[c, :, nx:] = side_ref[0, c]
+
+    def centre(a):
+        return a[0:ny, 0:nx]
+
+    def east(a):
+        return centre(pltpu.roll(a, a.shape[1] - 1, 1))
+
+    def west(a):
+        return centre(pltpu.roll(a, 1, 1))
+
+    def north(a):
+        return centre(pltpu.roll(a, a.shape[0] - 1, 0))
+
+    def south(a):
+        return centre(pltpu.roll(a, 1, 0))
+
+    temper = ext_ref[0]
+    saline = ext_ref[1]
+    density = BETA * saline - ALPHA * temper
+    cum = cum_ref[...] + density
+    cum_ref[...] = cum
+    pressure = GRAV_DZ * (cum - 0.5 * density)
+    grad_east = 0.5 * (east(pressure) - west(pressure))
+    grad_north = 0.5 * (north(pressure) - south(pressure))
+    eastward = ext_ref[2]
+    northward = ext_ref[3]
+    cor = cor_ref[...]
+    outs = (ot_ref, os_ref, ou_ref, ov_ref)
+    for c in range(4):
+        field = ext_ref[c]
+        lap = _lap(field)
+        bil = (north(lap) + south(lap) + east(lap) + west(lap) - 4.0 * centre(lap))
+        mixing = VISC_TWO * centre(lap) - VISC_FOUR * bil
+        if c < 2:
+            fe = field * eastward
+            fn = field * northward
+            adv = 0.5 * (east(fe) - west(fe)) + 0.5 * (north(fn) - south(fn))
+            forcing = -adv
+        elif c == 2:
+            forcing = cor * centre(northward) - grad_east
+        else:
+            forcing = -cor * centre(eastward) - grad_north
+        outs[c][0] = wet * (centre(field) + DT_STEP * (forcing + mixing))
+
+
+def stencil_call(levels, cor, fields, rows, side):
+    nz, ny, nx = fields[0].shape
+    plane = pl.BlockSpec((1, ny, nx), lambda k: (k, 0, 0))
+    fixed = pl.BlockSpec((ny, nx), lambda k: (0, 0))
+    out_shape = [jax.ShapeDtypeStruct((nz, ny, nx), jnp.float32)] * 4
+    return pl.pallas_call(
+        _step_kernel,
+        grid=(nz,),
+        in_specs=[fixed, fixed, plane, plane, plane, plane,
+                  pl.BlockSpec((1, 4, RING_ROWS - ny, nx), lambda k: (k, 0, 0, 0)),
+                  pl.BlockSpec((1, 4, RING_ROWS, RING_COLS), lambda k: (k, 0, 0, 0))],
+        out_specs=[plane] * 4,
+        out_shape=out_shape,
+        scratch_shapes=[pltpu.VMEM((4, RING_ROWS, nx + RING_COLS), jnp.float32),
+                        pltpu.VMEM((RING_ROWS, nx + RING_COLS), jnp.float32)],
+        compiler_params=pltpu.CompilerParams(dimension_semantics=("arbitrary",)),
+    )(levels, cor, *fields, rows, side)
+
+
+def pack_halo(from_south, north_rows, west, east):
+    nc, nz, _, nx = from_south.shape
+    gap = RING_ROWS - 16 - 4
+    rows = jnp.concatenate(
+        [north_rows, jnp.zeros((nc, nz, gap, nx), jnp.float32), from_south], axis=2)
+    def circ(col):
+        return jnp.concatenate(
+            [col[:, :, 2:], jnp.zeros((nc, nz, RING_ROWS - col.shape[2], 2), jnp.float32), col[:, :, :2]],
+            axis=2)
+    side = jnp.concatenate(
+        [circ(east), jnp.zeros((nc, nz, RING_ROWS, RING_COLS - 4), jnp.float32), circ(west)], axis=3)
+    return jnp.swapaxes(rows, 0, 1), jnp.swapaxes(side, 0, 1)
+
+
 def shift_pairs(count, step, wrap):
     pairs = []
     for i in range(count):
@@ -86,25 +195,22 @@
     submerged_layer_total,
     computed_block_flags,
 ):
+    raw = (thermal_anomaly, saltiness_anomaly, zonal_velocity_array, meridional_velocity_array)
     block_depth_layers = thermal_anomaly.shape[0]
     block_meridional_extent = thermal_anomaly.shape[1]
     n_lon = lax.axis_size("lon")
     n_lat = lax.axis_size("lat")
     tile_alive = computed_block_flags[0, 0] == 1
+    levels = jnp.where((seawater_profile_flags == 1) & tile_alive, submerged_layer_total, 0)
     depth_index = jnp.arange(block_depth_layers, dtype=jnp.int32)[:, None, None]
-    submerged_share = (
-        (depth_index < submerged_layer_total[None])
-        & (seawater_profile_flags[None] == 1)
-        & tile_alive
-    ).astype(jnp.float32)
-    fields = (
-        jnp.stack(
-            [thermal_anomaly, saltiness_anomaly, zonal_velocity_array, meridional_velocity_array]
-        )
-        * submerged_share
-    )
-    top = fields[:, :, -2:, :]
-    bottom = fields[:, :, :2, :]
+
+    def masked(rows, cols):
+        wet = (depth_index < levels[None, rows, cols]).astype(jnp.float32)
+        return jnp.stack([f[:, rows, cols] for f in raw]) * wet
+
+    every = slice(None)
+    top = masked(slice(-2, None), every)
+    bottom = masked(slice(0, 2), every)
     from_south = lax.ppermute(top, "lat", shift_pairs(n_lat, 1, False))
     from_north = lax.ppermute(bottom, "lat", shift_pairs(n_lat, -1, False))
     last = n_lat - 1
@@ -114,18 +220,22 @@
     fold_rows = folded[:, :, ::-1, ::-1] * signs
     is_northern = lax.axis_index("lat") == last
     north = jnp.where(is_northern, fold_rows, from_north)
-    tall = jnp.concatenate([from_south, fields, north], axis=2)
-    west = lax.ppermute(tall[..., -2:], "lon", shift_pairs(n_lon, 1, True))
-    east = lax.ppermute(tall[..., :2], "lon", shift_pairs(n_lon, -1, True))
-    extended = jnp.concatenate([west, tall, east], axis=3)
+
+    def tall(cols):
+        return jnp.concatenate(
+            [from_south[..., cols], masked(every, cols), north[..., cols]], axis=2)
+
+    west = lax.ppermute(tall(slice(-2, None)), "lon", shift_pairs(n_lon, 1, True))
+    east = lax.ppermute(tall(slice(0, 2)), "lon", shift_pairs(n_lon, -1, True))
+    rows, side = pack_halo(from_south, north, west, east)
     total_rows = block_meridional_extent * n_lat
     row_pos = (
         lax.axis_index("lat") * block_meridional_extent
         + jnp.arange(block_meridional_extent, dtype=jnp.int32)
     ).astype(jnp.float32)
     coriolis = (CORIOLIS_MAX * jnp.sin(jnp.pi * ((row_pos + 0.5) / total_rows - 0.5)))[:, None]
-    updated = update_fields(extended, submerged_share, coriolis)
-    return (updated[0], updated[1], updated[2], updated[3])
+    cor = jnp.broadcast_to(coriolis, levels.shape)
+    return tuple(stencil_call(levels, cor, raw, rows, side))
 
 
 def solution(mesh):

time: 166 us -> 87.3 us (0.53)
  other arithmetic: 78.8 us -> 7.04 us
  Pallas kernels: 0 us -> 26.1 us
  local copies, waits for them, and re-layouts: 47.5 us -> 24.7 us
  waiting for transfers between devices: 15.3 us -> 4.28 us
    sub x1 -> x0, other arithmetic: 29.1 us -> none  [laplace(): field[..., 2:, 1:-1] + field[..., :-2, 1:-1] + field[..., 1:-1, 2:]]
    pallas_call x0 -> x1, Pallas kernels: none -> 26.1 us  [stencil_call(): pl.pallas_call(_step_kernel, grid=(nz,), in_specs=[fixed, fixed, plane, p...]
    mul x3 -> x4, other arithmetic: 21.8 us -> 1.01 us  [masked(): return jnp.stack([f[:, rows, cols] for f in raw]) * wet]
    neg x1 -> x0, other arithmetic: 14.4 us -> none  [update_fields(): -advection]
    concatenate x1 -> x2, local copies, waits for them, and re-layouts: 13.7 us -> 0.15 us  [the longest x1 0.08 us: pack_halo(): jnp.concatenate([north_rows, jnp.zeros((nc, nz, gap, nx), jnp.float32), f...]
    ppermute x1, waiting for transfers between devices: 15.3 us -> 4.27 us  [per_device(): folded = lax.ppermute(top, ('lon', 'lat'), fold_pairs)]
    mul x1 -> x2, local copies, waits for them, and re-layouts: 5.94 us -> 0.09 us  [masked(): return jnp.stack([f[:, rows, cols] for f in raw]) * wet]
    broadcast_in_dim x1 -> x0, other arithmetic: 5.74 us -> none  [update_fields(): accel_east[None]]
  transfers between devices with their start and end apart: 5 -> 5, of which waited for: 1 -> 1; matrix products, arithmetic and copies ran while one was open for 6% -> 24% of each run, Pallas kernels for 0% -> 0%
where the time goes in v2:
time: 87.3 us; the launch traced here: 86.1 us
  Pallas kernels  26.1 us (30%)
  local copies, waits for them, and re-layouts  24.7 us (28%)
  starting transfers between devices  22.3 us (26%)
  other arithmetic  7.04 us (8%)
  waiting for transfers between devices  4.28 us (5%)
  between operations  1.66 us (2%)
    pallas_call x1, Pallas kernels, stencil_call(): pl.pallas_call(_step_kernel, grid=(nz,), in_specs=[fixed, fixed, plane, p...  26.1 us
    ppermute x1, starting transfers between devices, per_device(): folded = lax.ppermute(top, ('lon', 'lat'), fold_pairs)  11.5 us
    ppermute x1, starting transfers between devices, per_device(): east = lax.ppermute(tall(slice(0, 2)), 'lon', shift_pairs(n_lon, -1, True))  7.25 us
    rev x1, local copies, waits for them, and re-layouts, per_device(): fold_rows = folded[:, :, ::-1, ::-1] * signs  5.6 us
    slice x4, local copies, waits for them, and re-layouts, masked(): return jnp.stack([f[:, rows, cols] for f in raw]) * wet  5.4 us
    unnamed x16, local copies, waits for them, and re-layouts  4.42 us
    ppermute x1, waiting for transfers between devices, per_device(): folded = lax.ppermute(top, ('lon', 'lat'), fold_pairs)  4.27 us
    transpose x2, other arithmetic, pack_halo(): return (jnp.swapaxes(rows, 0, 1), jnp.swapaxes(side, 0, 1))  4.16 us
  transfers between devices with their start and end apart: 5, of which 1 were waited for; matrix products, arithmetic and copies ran while one was open for 24% of the time, Pallas kernels for 0%

profile of v2, /device:TPU:3, one launch (start us, length us, event | category | flops | bytes accessed | tf_op | source)
XLA Modules:
  0.0 86.1 jit_solution(12596417884728069755)
XLA Ops:
  1.4 0.9 %and_select_fusion.levels_ref = s32[16,1024]{1,0:T(8,128)S(1)} fusion(s32[16,1024]{1,0:T(8,128)} %param.13, s32[16,1024]{1,0:T(8,128)} %param.12, pred[]{:T(512)} %bitcast), kind=kLoop, calls=%fused_computation.19 | loop fusion | flops 49152 | bytes 196609 | tf_op jit(solution)/shard_map/jit(_where)/select_n | solution.py:204
  2.4 2.3 %slice_bitcast_fusion.2 = (f32[1,25,2,1024]{3,2,0,1:T(2,128)S(1)}, f32[1,25,2,1024]{3,2,0,1:T(2,128)S(1)}, f32[1,25,2,1024]{3,2,0,1:T(2,128)S(1)}, f32[1,25,2,1024]{3,2,0,1:T(2,128)S(1)}) fusion(f32[25,16,1024]{2,1,0:T(8,128)} %s_ref.1, f32[25,16,1024]{2,1,0:T(8,128)} %t_ref.1), kind=kLoop, calls=%fused_computation.9 | loop fusion | bytes 1638400 | tf_op jit(solution)/shard_map/stack | solution.py:209
  4.7 1.8 %slice_bitcast_fusion = (f32[1,25,2,1024]{3,2,0,1:T(2,128)S(1)}, f32[1,25,2,1024]{3,2,0,1:T(2,128)S(1)}, f32[1,25,2,1024]{3,2,0,1:T(2,128)S(1)}, f32[1,25,2,1024]{3,2,0,1:T(2,128)S(1)}) fusion(f32[25,16,1024]{2,1,0:T(8,128)} %v_ref.1, f32[25,16,1024]{2,1,0:T(8,128)S(1)} %copy-done), kind=kLoop, calls=%fused_computation.7 | loop fusion | bytes 1638400 | tf_op jit(solution)/shard_map/stack | solution.py:209
  7.0 1.3 %collective-permute-start.2 = (f32[4,25,2,1024]{3,2,0,1:T(2,128)S(1)}, f32[4,25,2,1024]{3,2,0,1:T(2,128)S(1)}, u32[]{:S(2)}, u32[]{:S(2)}) collective-permute-start(f32[4,25,2,1024]{3,2,0,1:T(2,128)S(1)} %maximum_multiply_fusion), channel_id=1, source_target_pairs={{0,1},{1,2},{2,3},{4,5},{5,6},{6,7},{8,9},{9,10},{10,11},{12,13},{... | collective-permute-start | bytes 2457608 | tf_op jit(solution)/shard_map/ppermute | solution.py:214
  8.3 11.5 %collective-permute-start = (f32[4,25,2,1024]{3,2,0,1:T(2,128)S(1)}, f32[4,25,2,1024]{3,2,0,1:T(2,128)}, u32[]{:S(2)}, u32[]{:S(2)}) collective-permute-start(f32[4,25,2,1024]{3,2,0,1:T(2,128)S(1)} %maximum_multiply_fusion), channel_id=1, source_target_pairs={{3,255},{7,251},{11,247},{15,243},{19,239},{23,235},{27,231},{31,2... | collective-permute-start | bytes 2457608 | tf_op jit(solution)/shard_map/ppermute | solution.py:218
  20.4 2.2 %collective-permute-start.1 = (f32[4,25,2,1024]{3,2,0,1:T(2,128)S(1)}, f32[4,25,2,1024]{3,2,0,1:T(2,128)}, u32[]{:S(2)}, u32[]{:S(2)}) collective-permute-start(f32[4,25,2,1024]{3,2,0,1:T(2,128)S(1)} %maximum_multiply_fusion.1), channel_id=1, source_target_pairs={{1,0},{2,1},{3,2},{5,4},{6,5},{7,6},{9,8},{10,9},{11,10},{13,12},{... | collective-permute-start | bytes 2457608 | tf_op jit(solution)/shard_map/ppermute | solution.py:215
  22.6 0.6 fusion.8
  23.2 1.2 %fusion.2 = (f32[25,16,2]{2,1,0:T(8,128)S(1)}, f32[25,16,2]{2,1,0:T(8,128)S(1)}) fusion(f32[25,16,1024]{2,1,0:T(8,128)} %t_ref.1), kind=kLoop, calls=%fused_computation.25 | loop fusion | bytes 12800 | tf_op jit(solution)/shard_map/slice | solution.py:209
  24.3 1.8 %fusion.3 = (f32[25,16,2]{2,1,0:T(8,128)}, f32[25,16,2]{2,1,0:T(8,128)S(1)}) fusion(f32[25,16,1024]{2,1,0:T(8,128)} %s_ref.1), kind=kLoop, calls=%fused_computation.26 | loop fusion | bytes 12800 | tf_op jit(solution)/shard_map/slice | solution.py:209
  26.1 0.7 fusion.4
  26.8 1.8 %fusion.5 = (f32[25,16,2]{2,1,0:T(8,128)}, f32[25,16,2]{2,1,0:T(8,128)S(1)}) fusion(f32[25,16,1024]{2,1,0:T(8,128)} %v_ref.1), kind=kLoop, calls=%fused_computation.28 | loop fusion | bytes 12800 | tf_op jit(solution)/shard_map/slice | solution.py:209
  28.9 1.1 %copy.55 = f32[25,16,2]{0,1,2:T(8,128)S(1)} copy(f32[25,16,2]{2,1,0:T(8,128)} %get-tuple-element.6) | data formatting | bytes 6400
  30.1 1.1 %copy.56 = f32[25,16,2]{0,1,2:T(8,128)S(1)} copy(f32[25,16,2]{2,1,0:T(8,128)} %get-tuple-element.8) | data formatting | bytes 6400
  31.2 1.1 %copy.57 = f32[25,16,2]{0,1,2:T(8,128)S(1)} copy(f32[25,16,2]{2,1,0:T(8,128)} %get-tuple-element.10) | data formatting | bytes 6400
  34.1 4.3 %collective-permute-done = f32[4,25,2,1024]{3,2,0,1:T(2,128)} collective-permute-done((f32[4,25,2,1024]{3,2,0,1:T(2,128)S(1)}, f32[4,25,2,1024]{3,2,0,1:T(2,128)}, u32[]{:S(2)}, u32[]{:S(2)}) %collective-permute-start) | collective-permute-done | bytes 819232 | tf_op jit(solution)/shard_map/ppermute | solution.py:218
  38.4 5.6 %rev.3 = f32[4,25,2,1024]{3,2,0,1:T(2,128)S(1)} reverse(f32[4,25,2,1024]{3,2,0,1:T(2,128)} %collective-permute-done), dimensions={2,3} | reverse | bytes 1638400 | tf_op jit(solution)/shard_map/rev | solution.py:220
  44.0 0.6 multiply_select_fusion
  45.2 7.3 %collective-permute-start.3 = (f32[4,25,20,2]{1,0,3,2:T(4,128)S(1)}, f32[4,25,20,2]{1,0,3,2:T(4,128)S(1)}, u32[]{:S(2)}, u32[]{:S(2)}) collective-permute-start(f32[4,25,20,2]{1,0,3,2:T(4,128)S(1)} %pad_maximum_fusion), channel_id=1, source_target_pairs={{0,252},{4,0},{8,4},{12,8},{16,12},{20,16},{24,20},{28,24},{32,28}... | collective-permute-start | bytes 48008 | tf_op jit(solution)/shard_map/ppermute | solution.py:229
  52.4 2.5 %maximum_bitcast_fusion.rows_ref = f32[25,4,8,1024]{3,2,1,0:T(8,128)} fusion(f32[4,25,2,1024]{3,2,0,1:T(2,128)S(1)} %collective-permute-done.2, f32[4,25,2,1024]{3,2,0,1:T(2,128)S(1)} %multiply_select_fusion, f32[8]{0:T(128)S(1)} %pad.22.clone), kind=kLoop, calls=%fused_computation | loop fusion | flops 1638400 | bytes 4915232 | tf_op jit(solution)/shard_map/transpose | solution.py:175
  55.3 1.2 %copy.42 = f32[4,25,18,2]{3,2,0,1:T(8,128)S(1)} copy(f32[4,25,18,2]{1,0,3,2:T(4,128)S(1)} %slice.117) | data formatting | bytes 28800 | tf_op jit(solution)/shard_map/slice | solution.py:171
  56.5 1.2 %copy.52 = f32[4,25,18,2]{3,2,0,1:T(8,128)S(1)} copy(f32[4,25,18,2]{1,0,3,2:T(4,128)S(1)} %slice.122) | data formatting | bytes 28800 | tf_op jit(solution)/shard_map/slice | solution.py:171
  57.7 1.7 %maximum_bitcast_fusion.1.side_ref = f32[25,4,24,128]{3,2,1,0:T(8,128)} fusion(f32[4,25,2,2]{3,2,0,1:T(2,128)S(1)} %copy.53, f32[4,25,4,2]{3,2,0,1:T(4,128)S(1)} %broadcast.73, f32[4,25,18,2]{3,2,0,1:T(8,128)S(1)} %copy.52, f32[4,25,2,2]{3,2,0,1:T(2,128)S(1)} %copy.43, f32[4,25,18,2]{3,2,0,1:T(8,128)S(1)} %copy.42, f32[128]{0:T(128)S(1)} %pad.3.clone), kind=kLoop, calls=%fused_computation.1 | loop fusion | flops 1843200 | bytes 1264512 | tf_op jit(solution)/shard_map/transpose | solution.py:175
  59.3 0.7 broadcast_in_dim.11.cor_ref
  60.0 26.1 %shard_map.111 = (f32[25,16,1024]{2,1,0:T(8,128)}, f32[25,16,1024]{2,1,0:T(8,128)}, f32[25,16,1024]{2,1,0:T(8,128)}, f32[25,16,1024]{2,1,0:T(8,128)}) custom-call(s32[16,1024]{1,0:T(8,128)} %copy-done.1, f32[16,1024]{1,0:T(8,128)} %broadcast_in_dim.11.cor_ref, f32[25,16,1024]{2,1,0:T(8,128)} %t_ref.1, f32[25,16,1024]{2,1,0:T(8,128)} %s_ref.1, ...), custom_call_target="tpu_custom_call" | custom-call | tf_op jit(solution)/shard_map/pallas_call | solution.py:150
  (51 shorter events, 4.2 us)
Async XLA Ops:
  0.6 4.1 %copy-start = (f32[25,16,1024]{2,1,0:T(8,128)S(1)}, f32[25,16,1024]{2,1,0:T(8,128)}, u32[]{:S(2)}) copy-start(f32[25,16,1024]{2,1,0:T(8,128)} %u_ref.1) | copy-start | bytes 4915204
  2.3 20.3 %copy-start.1 = (s32[16,1024]{1,0:T(8,128)}, s32[16,1024]{1,0:T(8,128)S(1)}, u32[]{:S(2)}) copy-start(s32[16,1024]{1,0:T(8,128)S(1)} %and_select_fusion.levels_ref) | copy-start | bytes 196612
  7.0 26.7 %collective-permute-start.2 = (f32[4,25,2,1024]{3,2,0,1:T(2,128)S(1)}, f32[4,25,2,1024]{3,2,0,1:T(2,128)S(1)}, u32[]{:S(2)}, u32[]{:S(2)}) collective-permute-start(f32[4,25,2,1024]{3,2,0,1:T(2,128)S(1)} %maximum_multiply_fusion), channel_id=1, source_target_pairs={{0,1},{1,2},{2,3},{4,5},{5,6},{6,7},{8,9},{9,10},{10,11},{12,13},{... | collective-permute-start | bytes 2457608 | tf_op jit(solution)/shard_map/ppermute | solution.py:214
  8.3 30.1 %collective-permute-start = (f32[4,25,2,1024]{3,2,0,1:T(2,128)S(1)}, f32[4,25,2,1024]{3,2,0,1:T(2,128)}, u32[]{:S(2)}, u32[]{:S(2)}) collective-permute-start(f32[4,25,2,1024]{3,2,0,1:T(2,128)S(1)} %maximum_multiply_fusion), channel_id=1, source_target_pairs={{3,255},{7,251},{11,247},{15,243},{19,239},{23,235},{27,231},{31,2... | collective-permute-start | bytes 2457608 | tf_op jit(solution)/shard_map/ppermute | solution.py:218
  20.4 23.6 %collective-permute-start.1 = (f32[4,25,2,1024]{3,2,0,1:T(2,128)S(1)}, f32[4,25,2,1024]{3,2,0,1:T(2,128)}, u32[]{:S(2)}, u32[]{:S(2)}) collective-permute-start(f32[4,25,2,1024]{3,2,0,1:T(2,128)S(1)} %maximum_multiply_fusion.1), channel_id=1, source_target_pairs={{1,0},{2,1},{3,2},{5,4},{6,5},{7,6},{9,8},{10,9},{11,10},{13,12},{... | collective-permute-start | bytes 2457608 | tf_op jit(solution)/shard_map/ppermute | solution.py:215
  23.2 5.4 %copy-start.2 = (s32[16,2]{1,0:T(8,128)S(1)}, s32[16,2]{1,0:T(8,128)}, u32[]{:S(2)}) copy-start(s32[16,2]{1,0:T(8,128)} %get-tuple-element.24) | copy-start | bytes 388
  32.8 11.2 %copy-start.3 = (f32[4]{0:T(128)S(1)}, f32[4]{0:T(128)}, u32[]{:S(2)}) copy-start(f32[4]{0:T(128)} %constant.32.clone) | copy-start | bytes 52
  45.1 10.0 %collective-permute-start.4 = (f32[4,25,20,2]{1,0,3,2:T(4,128)S(1)}, f32[4,25,20,2]{1,0,3,2:T(4,128)S(1)}, u32[]{:S(2)}, u32[]{:S(2)}) collective-permute-start(f32[4,25,20,2]{1,0,3,2:T(4,128)S(1)} %pad_maximum_fusion.1), channel_id=1, source_target_pairs={{0,4},{4,8},{8,12},{12,16},{16,20},{20,24},{24,28},{28,32},{32,36}... | collective-permute-start | bytes 48008 | tf_op jit(solution)/shard_map/ppermute | solution.py:228
  45.2 9.7 %collective-permute-start.3 = (f32[4,25,20,2]{1,0,3,2:T(4,128)S(1)}, f32[4,25,20,2]{1,0,3,2:T(4,128)S(1)}, u32[]{:S(2)}, u32[]{:S(2)}) collective-permute-start(f32[4,25,20,2]{1,0,3,2:T(4,128)S(1)} %pad_maximum_fusion), channel_id=1, source_target_pairs={{0,252},{4,0},{8,4},{12,8},{16,12},{20,16},{24,20},{28,24},{32,28}... | collective-permute-start | bytes 48008 | tf_op jit(solution)/shard_map/ppermute | solution.py:229
